TPU v7x, 128 devices: a whole 4x4x4 slice. The times are simulated.
128 devices in a mesh: pb: 8 (over z, y_lo), kv: 16 (over x, y_hi, core).
Axes of the slice: x: 4, y: 4 (y_hi: 2, y_lo: 2; y = y_hi * 2 + y_lo), z: 4, core: 2. Of those that a mesh axis runs over, the one named last changes fastest.
Arguments:
- slab_start: int32 [1], replicated, may hold values from 0 to 12288
- queries: bfloat16 [4096, 4096], P('pb', 'kv'), may hold values from -6 to 6
- keys: bfloat16 [16384, 2048], P('kv'), may hold values from -6 to 6
- values: bfloat16 [16384, 2048], P('kv'), may hold values from -6 to 6
- out_weight: bfloat16 [4096, 4608], P('kv'), may hold values from -0.09375 to 0.09375
Outputs:
- projected: float32 [4096, 4608], P(('pb', 'kv'))
Inputs may be any that keep to these rules, and one draw needn't show every extreme that they name: The slab lies inside the context: slab_start + 4096 <= 16384.
All inputs are finite; a program needn't handle non-finite values.
Results may differ from a plain program's by a relative error of at most 0.01.
Values may be sent and summed in bfloat16 or wider, within the bound.
No kernel may reach another device: no remote copies, remote signals or barrier semaphores. Data moves between devices by JAX's collectives and lax.ppermute only.
A program may use at most 128 MiB of HBM per device.

v0:
```python
import jax
import jax.numpy as jnp
from jax import lax
from jax.sharding import PartitionSpec as P

HQ = 32
KVH = 16
HD = 128
CAP = 50
SCALAR = 144


def attend_block(carry, q_block, q_pos, key_part, value_part, key_pos):
    top, total, summed = carry
    raw = jnp.einsum("gqd,kgd->gqk", q_block, key_part, preferred_element_type=jnp.float32)
    scores = CAP * jnp.tanh(raw * SCALAR ** (-0.5) / CAP)
    kept = key_pos[None, None, :] <= q_pos[None, :, None]
    scores = jnp.where(kept, scores, -1e30)
    new_top = jnp.maximum(top, jnp.max(scores, axis=2))
    keep = jnp.exp(top - new_top)
    prob = jnp.where(kept, jnp.exp(scores - new_top[:, :, None]), 0.0)
    total = total * keep + jnp.sum(prob, axis=2)
    weights = prob.astype(jnp.bfloat16)
    summed = summed * keep[:, :, None] + jnp.einsum(
        "gqk,kgd->gqd", weights, value_part, preferred_element_type=jnp.float32
    )
    return (new_top, total, summed)


def empty_state(heads, rows):
    return (
        jnp.full((heads, rows), -1e30, jnp.float32),
        jnp.zeros((heads, rows), jnp.float32),
        jnp.zeros((heads, rows, HD), jnp.float32),
    )


def by_heads(queries, keys, values, positions):
    n_kv = lax.axis_size("kv")
    group = HQ // KVH
    rows_dev = queries.shape[0]
    key_dev = keys.shape[0]
    kv_feat = keys.shape[1] // n_kv
    pair = (keys.reshape(key_dev, n_kv, kv_feat), values.reshape(key_dev, n_kv, kv_feat))
    key_all, value_all = (
        lax.all_to_all(pair[0], "kv", split_axis=1, concat_axis=0, tiled=True),
        lax.all_to_all(pair[1], "kv", split_axis=1, concat_axis=0, tiled=True),
    )
    context = key_all.shape[0]
    kv_local = kv_feat // HD
    tile = min(256, rows_dev)
    tiles = rows_dev // tile
    width = min(2048, context)
    q_tiles = queries.reshape(tiles, tile, kv_local, group, HD)
    p_tiles = positions.reshape(tiles, tile)

    def one_tile(item):
        q_block, pos = item
        q_block = q_block.transpose(1, 0, 2, 3).reshape(kv_local, tile * group, HD)
        q_pos = jnp.repeat(pos, group)
        count = jnp.max(pos) // width + 1

        def step(index, carry):
            key_part = lax.dynamic_slice_in_dim(key_all, index * width, width, 0)
            value_part = lax.dynamic_slice_in_dim(value_all, index * width, width, 0)
            key_pos = index * width + jnp.arange(width, dtype=jnp.int32)
            return attend_block(carry, q_block, q_pos, key_part, value_part, key_pos)

        top, total, summed = lax.fori_loop(0, count, step, empty_state(kv_local, tile * group))
        mixed = (summed / total[:, :, None]).astype(jnp.bfloat16)
        return (
            mixed.reshape(kv_local, tile, group, HD)
            .transpose(1, 0, 2, 3)
            .reshape(tile, kv_local * group * HD)
        )

    result = lax.map(one_tile, (q_tiles, p_tiles))
    return result.reshape(rows_dev, kv_local * group * HD)


def per_device(slab_start, queries, keys, values, out_weight):
    rows_dev = queries.shape[0]
    first = slab_start[0]
    row_index = jnp.arange(rows_dev, dtype=jnp.int32)
    anchor = lax.axis_index("pb") * rows_dev + row_index
    positions = first + anchor
    attended = by_heads(queries, keys, values, positions)
    return lax.psum_scatter(
        jnp.dot(attended, out_weight, preferred_element_type=jnp.float32),
        "kv",
        scatter_dimension=0,
        tiled=True,
    )


def solution(mesh):
    in_specs = (P(), P("pb", "kv"), P("kv", None), P("kv", None), P("kv", None))
    out_specs = P(("pb", "kv"), None)
    return jax.shard_map(
        per_device, mesh=mesh, in_specs=in_specs, out_specs=out_specs, check_vma=False
    )
```

profile of v0, /device:TPU:120, one launch (start us, length us, event | category | flops | bytes accessed | tf_op | source)
XLA Modules:
  0.0 360.0 jit_solution(16155916015129229009)
XLA Ops:
  6.5 6.6 %copy.10 = bf16[1024,2048]{0,1:T(8,128)(2,1)} copy(bf16[1024,2048]{1,0:T(8,128)(2,1)} %param.12) | data formatting | bytes 8388608 | tf_op args[3]
  13.1 7.3 %all-to-all-start.1 = ((bf16[1024,16,128]{0,2,1:T(8,128)(2,1)}), bf16[1024,16,128]{0,2,1:T(8,128)(2,1)}, u32[]{:S(2)}, u32[]{:S(2)}) async-start(bf16[1024,16,128]{0,2,1:T(8,128)(2,1)} %bitcast.66), calls=%async_computation.1 | async-start | bytes 8388608 | tf_op jit(solution)/shard_map/all_to_all | solution.py:47
  20.4 6.4 %copy.8 = bf16[1024,2048]{0,1:T(8,128)(2,1)} copy(bf16[1024,2048]{1,0:T(8,128)(2,1)} %param.11) | data formatting | bytes 8388608 | tf_op args[2]
  26.8 50.8 %all-to-all-done.1 = bf16[1024,16,128]{0,2,1:T(8,128)(2,1)} async-done(((bf16[1024,16,128]{0,2,1:T(8,128)(2,1)}), bf16[1024,16,128]{0,2,1:T(8,128)(2,1)}, u32[]{:S(2)}, u32[]{:S(2)}) %all-to-all-start.1) | async-done | bytes 4194336 | tf_op jit(solution)/shard_map/all_to_all | solution.py:47
  77.6 9.3 %all-to-all-start = ((bf16[1024,16,128]{0,2,1:T(8,128)(2,1)}), bf16[1024,16,128]{0,2,1:T(8,128)(2,1)}, u32[]{:S(2)}, u32[]{:S(2)}) async-start(bf16[1024,16,128]{0,2,1:T(8,128)(2,1)} %bitcast.65), calls=%async_computation | async-start | bytes 8388608 | tf_op jit(solution)/shard_map/all_to_all | solution.py:46
  87.7 6.4 %copy.11 = bf16[16,1024,1,128]{3,1,0,2:T(8,128)(2,1)} copy(bf16[16,1024,1,128]{1,3,0,2:T(8,128)(2,1)} %bitcast.10) | data formatting | bytes 8388608 | tf_op jit(solution)/shard_map/all_to_all | solution.py:47
  94.1 50.0 %all-to-all-done = bf16[1024,16,128]{0,2,1:T(8,128)(2,1)} async-done(((bf16[1024,16,128]{0,2,1:T(8,128)(2,1)}), bf16[1024,16,128]{0,2,1:T(8,128)(2,1)}, u32[]{:S(2)}, u32[]{:S(2)}) %all-to-all-start) | async-done | bytes 4194336 | tf_op jit(solution)/shard_map/all_to_all | solution.py:46
  144.1 6.4 %copy.9 = bf16[16,1024,1,128]{3,1,0,2:T(8,128)(2,1)} copy(bf16[16,1024,1,128]{1,3,0,2:T(8,128)(2,1)} %bitcast.6) | data formatting | bytes 8388608 | tf_op jit(solution)/shard_map/all_to_all | solution.py:46
  150.5 89.1 %while.40 = (s32[]{:T(128)}, bf16[2,256,256]{2,1,0:T(8,128)(2,1)S(1)}, s32[2,256]{1,0:T(2,128)S(1)}, bf16[2,256,1,2,128]{4,3,1,2,0:T(2,128)(2,1)S(1)}, bf16[1638...) while((s32[]{:T(128)}, ...), condition=%wide.region_6.7_spmd, body=%wide.region_0.6_spmd.sunk | while | flops 550767872 | bytes 15816322 | solution.py:77
  153.8 41.0 %while.41 = (s32[]{:T(128)}, f32[1,512]{1,0:T(1,128)S(1)}, f32[1,512]{1,0:T(1,128)S(1)}, f32[1,512,128]{2,1,0:T(8,128)S(1)}, s32[]{:T(128)}, /*index=5*/bf16[163...) while((s32[]{:T(128)}, f32[1,512]{1,0:T(1,128)S(1)}, ...), condition=%wide.region_5.5_spmd.clone, body=%wide.region_2.4_spmd.clone.sunk | while | flops 550636544 | bytes 14365879 | solution.py:69
  154.1 2.2 fusion.35
  157.2 2.4 fusion.37
  160.0 2.2 fusion.35
  163.1 2.4 fusion.37
  169.0 2.4 fusion.37
  174.8 2.4 fusion.37
  177.5 2.2 fusion.35
  180.7 2.4 fusion.37
  186.5 2.4 fusion.37
  192.4 2.4 fusion.37
  198.4 41.0 %while.41 = (s32[]{:T(128)}, f32[1,512]{1,0:T(1,128)S(1)}, f32[1,512]{1,0:T(1,128)S(1)}, f32[1,512,128]{2,1,0:T(8,128)S(1)}, s32[]{:T(128)}, /*index=5*/bf16[163...) while((s32[]{:T(128)}, f32[1,512]{1,0:T(1,128)S(1)}, ...), condition=%wide.region_5.5_spmd.clone, body=%wide.region_2.4_spmd.clone.sunk | while | flops 550636544 | bytes 14365879 | solution.py:69
  201.8 2.4 fusion.37
  204.5 2.2 fusion.35
  207.7 2.4 fusion.37
  213.5 2.4 fusion.37
  219.4 2.4 fusion.37
  225.2 2.4 fusion.37
  231.1 2.4 fusion.37
  233.8 2.2 fusion.35
  236.9 2.4 fusion.37
  239.7 5.0 %fusion.23 = f32[512,4608]{1,0:T(8,128)} fusion(bf16[512,256]{1,0:T(8,128)(2,1)S(1)} %bitcast.75, bf16[256,4608]{1,0:T(8,128)(2,1)S(1)} %copy-done), kind=kOutput, calls=%fused_computation.27 | convolution fusion | flops 1207959552 | bytes 12058624 | tf_op jit(solution)/shard_map/dot_general | solution.py:89
  244.7 108.5 %reduce-scatter.2.cloned.1.call-done = f32[32,4608]{1,0:T(8,128)} async-done(((f32[512,4608]{1,0:T(8,128)}), f32[32,4608]{1,0:T(8,128)}) %reduce-scatter.2.cloned.1.call-update) | async-done | bytes 589840 | tf_op jit(solution)/shard_map/reduce_scatter | solution.py:88
  (132 shorter events, 37.9 us)
Async XLA Ops:
  6.5 233.1 %copy-start = (bf16[256,4608]{1,0:T(8,128)(2,1)S(1)}, bf16[256,4608]{1,0:T(8,128)(2,1)}, u32[]{:S(2)}) copy-start(bf16[256,4608]{1,0:T(8,128)(2,1)} %param.13) | copy-start | bytes 7077892
  13.1 64.5 %all-to-all-start.1 = ((bf16[1024,16,128]{0,2,1:T(8,128)(2,1)}), bf16[1024,16,128]{0,2,1:T(8,128)(2,1)}, u32[]{:S(2)}, u32[]{:S(2)}) async-start(bf16[1024,16,128]{0,2,1:T(8,128)(2,1)} %bitcast.66), calls=%async_computation.1 | async-start | bytes 8388608 | tf_op jit(solution)/shard_map/all_to_all | solution.py:47
  77.6 9.4 %copy-start.1 = (bf16[512,256]{1,0:T(8,128)(2,1)S(1)}, bf16[512,256]{1,0:T(8,128)(2,1)}, u32[]{:S(2)}) copy-start(bf16[512,256]{1,0:T(8,128)(2,1)} %param.10) | copy-start | bytes 786436
  77.6 66.5 %all-to-all-start = ((bf16[1024,16,128]{0,2,1:T(8,128)(2,1)}), bf16[1024,16,128]{0,2,1:T(8,128)(2,1)}, u32[]{:S(2)}, u32[]{:S(2)}) async-start(bf16[1024,16,128]{0,2,1:T(8,128)(2,1)} %bitcast.65), calls=%async_computation | async-start | bytes 8388608 | tf_op jit(solution)/shard_map/all_to_all | solution.py:46
  86.9 266.3 %reduce-scatter.2.cloned.1.call-start = ((), (), s32[]{:S(2)}) async-start(), calls=%async_computation.3 | async-start | bytes 10027008 | tf_op jit(solution)/shard_map/reduce_scatter | solution.py:88
Sparse Core Ops, SparseCore 0:
  244.8 108.3 reduce-scatter.1
where the time goes:
time: 365 us; the launch traced here: 360 us
  waiting for transfers between devices  209 us (57%)
  matrix products  69.7 us (19%)
  local copies, waits for them, and re-layouts  29.5 us (8%)
  starting transfers between devices  16.7 us (5%)
  other arithmetic  14.6 us (4%)
  between operations  14.1 us (4%)
  loops' own time  6.25 us (2%)
    reduce_scatter x1, waiting for transfers between devices, per_device(): lax.psum_scatter(jnp.dot(attended, out_weight, preferred_element_type=jnp...  108 us
    all_to_all x1, waiting for transfers between devices, by_heads(): lax.all_to_all(pair[1], 'kv', split_axis=1, concat_axis=0, tiled=True)  50.8 us
    all_to_all x1, waiting for transfers between devices, by_heads(): lax.all_to_all(pair[0], 'kv', split_axis=1, concat_axis=0, tiled=True)  50 us
    dot_general x14, matrix products, attend_block(): jnp.einsum('gqk,kgd->gqd', weights, value_part, preferred_element_type=jn...  34.1 us
    dot_general x14, matrix products, attend_block(): jnp.einsum('gqd,kgd->gqk', q_block, key_part, preferred_element_type=jnp....  30.5 us
    unnamed x6, local copies, waits for them, and re-layouts  13 us
    reduce_sum x14, other arithmetic, attend_block(): total = total * keep + jnp.sum(prob, axis=2)  12.6 us
    all_to_all x1, starting transfers between devices, by_heads(): lax.all_to_all(pair[0], 'kv', split_axis=1, concat_axis=0, tiled=True)  9.34 us
  transfers between devices with their start and end apart: 3, of which 3 were waited for; matrix products, arithmetic and copies ran while one was open for 4% of the time, Pallas kernels for 0%

commit v1 on v0

--- a/solution.py
+++ b/solution.py
@@ -1,13 +1,14 @@
 import jax
 import jax.numpy as jnp
 from jax import lax
-from jax.sharding import PartitionSpec as P
+from jax.sharding import Mesh, PartitionSpec as P
 
 HQ = 32
 KVH = 16
 HD = 128
 CAP = 50
 SCALAR = 144
+KV = ("kx", "kc")
 
 
 def attend_block(carry, q_block, q_pos, key_part, value_part, key_pos):
@@ -36,16 +37,17 @@
 
 
 def by_heads(queries, keys, values, positions):
-    n_kv = lax.axis_size("kv")
+    n_kv = lax.axis_size(KV)
     group = HQ // KVH
     rows_dev = queries.shape[0]
     key_dev = keys.shape[0]
     kv_feat = keys.shape[1] // n_kv
-    pair = (keys.reshape(key_dev, n_kv, kv_feat), values.reshape(key_dev, n_kv, kv_feat))
-    key_all, value_all = (
-        lax.all_to_all(pair[0], "kv", split_axis=1, concat_axis=0, tiled=True),
-        lax.all_to_all(pair[1], "kv", split_axis=1, concat_axis=0, tiled=True),
-    )
+    pair = jnp.stack(
+        (keys.reshape(key_dev, n_kv, kv_feat), values.reshape(key_dev, n_kv, kv_feat)), axis=0
+    ).transpose(2, 0, 1, 3)
+    both = lax.all_to_all(pair, KV, split_axis=0, concat_axis=0, tiled=True)
+    key_all = both[:, 0].reshape(n_kv * key_dev, kv_feat // HD, HD)
+    value_all = both[:, 1].reshape(n_kv * key_dev, kv_feat // HD, HD)
     context = key_all.shape[0]
     kv_local = kv_feat // HD
     tile = min(256, rows_dev)
@@ -85,17 +87,25 @@
     anchor = lax.axis_index("pb") * rows_dev + row_index
     positions = first + anchor
     attended = by_heads(queries, keys, values, positions)
-    return lax.psum_scatter(
-        jnp.dot(attended, out_weight, preferred_element_type=jnp.float32),
-        "kv",
-        scatter_dimension=0,
-        tiled=True,
+    partial = jnp.dot(attended, out_weight, preferred_element_type=jnp.float32)
+    n_chip = lax.axis_size("kx")
+    n_core = lax.axis_size("kc")
+    partial = partial.reshape(n_chip, n_core, rows_dev // (n_chip * n_core), partial.shape[1])
+    core = lax.axis_index("kc")
+    mine = lax.dynamic_index_in_dim(partial, core, 1, keepdims=False)
+    theirs = lax.dynamic_index_in_dim(partial, 1 - core, 1, keepdims=False)
+    on_chip = mine + lax.ppermute(theirs, "kc", [(0, 1), (1, 0)])
+    parts = lax.all_to_all(
+        on_chip.astype(jnp.bfloat16), "kx", split_axis=0, concat_axis=0, tiled=True
     )
+    return jnp.sum(parts.astype(jnp.float32), axis=0)
 
 
 def solution(mesh):
-    in_specs = (P(), P("pb", "kv"), P("kv", None), P("kv", None), P("kv", None))
-    out_specs = P(("pb", "kv"), None)
+    n_pb, n_kv = mesh.devices.shape
+    split = Mesh(mesh.devices.reshape(n_pb, n_kv // 2, 2), ("pb", "kx", "kc"))
+    in_specs = (P(), P("pb", KV), P(KV, None), P(KV, None), P(KV, None))
+    out_specs = P(("pb",) + KV, None)
     return jax.shard_map(
-        per_device, mesh=mesh, in_specs=in_specs, out_specs=out_specs, check_vma=False
+        per_device, mesh=split, in_specs=in_specs, out_specs=out_specs, check_vma=False
     )

time: 365 us -> 315 us (0.86)
  waiting for transfers between devices: 209 us -> 130 us
  blocking collectives: 0 us -> 45.9 us
  matrix products: 69.7 us -> 47.5 us
  local copies, waits for them, and re-layouts: 29.5 us -> 47.8 us
  between operations: 14.1 us -> 0.72 us
  other arithmetic: 14.6 us -> 23.7 us
  starting transfers between devices: 16.7 us -> 7.81 us
    reduce_scatter x1 -> x0, waiting for transfers between devices: 108 us -> none  [per_device(): lax.psum_scatter(jnp.dot(attended, out_weight, preferred_element_type=jnp...]
    all_to_all x0 -> x1, blocking collectives: none -> 45.9 us  [per_device(): lax.all_to_all(on_chip.astype(jnp.bfloat16), 'kx', split_axis=0, concat_a...]
    all_to_all x2 -> x1, waiting for transfers between devices: 101 us -> 122 us  [by_heads(): both = lax.all_to_all(pair, KV, split_axis=0, concat_axis=0, tiled=True)]
    unnamed x6 -> x10, local copies, waits for them, and re-layouts: 13 us -> 28 us
    all_to_all x2 -> x0, local copies, waits for them, and re-layouts: 12.8 us -> none  [the longest x1 6.41 us: by_heads(): lax.all_to_all(pair[0], 'kv', split_axis=1, concat_axis=0, tiled=True)]
    dot_general x14 -> x10, matrix products: 34.1 us -> 24.4 us  [attend_block(): jnp.einsum('gqk,kgd->gqd', weights, value_part, preferred_element_type=jn...]
    all_to_all x2 -> x1, starting transfers between devices: 16.6 us -> 7.41 us  [by_heads(): both = lax.all_to_all(pair, KV, split_axis=0, concat_axis=0, tiled=True)]
    dot_general x14 -> x10, matrix products: 30.5 us -> 21.8 us  [attend_block(): jnp.einsum('gqd,kgd->gqk', q_block, key_part, preferred_element_type=jnp....]
  transfers between devices with their start and end apart: 3 -> 2, of which waited for: 3 -> 2; matrix products, arithmetic and copies ran while one was open for 4% -> 0% of each run, Pallas kernels for 0% -> 0%
where the time goes in v1:
time: 315 us; the launch traced here: 309 us
  waiting for transfers between devices  130 us (41%)
  local copies, waits for them, and re-layouts  47.8 us (15%)
  matrix products  47.5 us (15%)
  blocking collectives  45.9 us (15%)
  other arithmetic  23.7 us (8%)
  starting transfers between devices  7.81 us (2%)
  loops' own time  5.95 us (2%)
    all_to_all x1, waiting for transfers between devices, by_heads(): both = lax.all_to_all(pair, KV, split_axis=0, concat_axis=0, tiled=True)  122 us
    all_to_all x1, blocking collectives, per_device(): lax.all_to_all(on_chip.astype(jnp.bfloat16), 'kx', split_axis=0, concat_a...  45.9 us
    unnamed x10, local copies, waits for them, and re-layouts  28 us
    dot_general x10, matrix products, attend_block(): jnp.einsum('gqk,kgd->gqd', weights, value_part, preferred_element_type=jn...  24.4 us
    dot_general x10, matrix products, attend_block(): jnp.einsum('gqd,kgd->gqk', q_block, key_part, preferred_element_type=jnp....  21.8 us
    reduce_sum x10, other arithmetic, attend_block(): total = total * keep + jnp.sum(prob, axis=2)  8.97 us
    transpose x1, local copies, waits for them, and re-layouts, by_heads(): pair = jnp.stack((keys.reshape(key_dev, n_kv, kv_feat), values.reshape(ke...  8.18 us
    ppermute x1, waiting for transfers between devices, per_device(): on_chip = mine + lax.ppermute(theirs, 'kc', [(0, 1), (1, 0)])  7.88 us
  transfers between devices with their start and end apart: 2, of which 2 were waited for; matrix products, arithmetic and copies ran while one was open for 0% of the time, Pallas kernels for 0%

profile of v1, /device:TPU:120, one launch (start us, length us, event | category | flops | bytes accessed | tf_op | source)
XLA Modules:
  0.0 309.0 jit_solution(16612353943164462954)
XLA Ops:
  0.0 6.6 %copy.12 = bf16[1024,2048]{0,1:T(8,128)(2,1)} copy(bf16[1024,2048]{1,0:T(8,128)(2,1)} %param.11) | data formatting | bytes 8388608 | tf_op args[2]
  6.6 6.4 %copy.13 = bf16[1024,2048]{0,1:T(8,128)(2,1)} copy(bf16[1024,2048]{1,0:T(8,128)(2,1)} %param.12) | data formatting | bytes 8388608 | tf_op args[3]
  13.0 7.4 %maximum_bitcast_fusion = bf16[16,2,1024,128]{2,3,0,1:T(8,128)(2,1)} fusion(bf16[1,1024,16,128]{1,3,2,0:T(8,128)(2,1)} %bitcast.72, bf16[1,1024,16,128]{1,3,2,0:T(8,128)(2,1)} %bitcast.71), kind=kLoop, calls=%fused_computation.24 | loop fusion | flops 4194304 | bytes 16777216 | tf_op jit(solution)/shard_map/transpose | solution.py:47
  20.4 8.2 %copy.14 = bf16[16,2,1024,128]{2,3,1,0:T(8,128)(2,1)} copy(bf16[16,2,1024,128]{2,3,0,1:T(8,128)(2,1)} %maximum_bitcast_fusion) | data formatting | bytes 16777216 | tf_op jit(solution)/shard_map/transpose | solution.py:47
  28.6 7.4 %all-to-all-start = ((bf16[16,2,1024,128]{2,3,1,0:T(8,128)(2,1)}), bf16[16,2,1024,128]{2,3,1,0:T(8,128)(2,1)}, u32[]{:S(2)}, u32[]{:S(2)}) async-start(bf16[16,2,1024,128]{2,3,1,0:T(8,128)(2,1)} %copy.14), calls=%async_computation | async-start | bytes 16777216 | tf_op jit(solution)/shard_map/all_to_all | solution.py:48
  36.8 121.7 %all-to-all-done = bf16[16,2,1024,128]{2,3,1,0:T(8,128)(2,1)} async-done(((bf16[16,2,1024,128]{2,3,1,0:T(8,128)(2,1)}), bf16[16,2,1024,128]{2,3,1,0:T(8,128)(2,1)}, u32[]{:S(2)}, u32[]{:S(2)}) %all-to-all-start) | async-done | bytes 8388640 | tf_op jit(solution)/shard_map/all_to_all | solution.py:48
  158.5 6.1 %fusion.26 = (bf16[16,1,1024,128]{2,3,1,0:T(8,128)(2,1)}, bf16[16,1,1024,128]{2,3,1,0:T(8,128)(2,1)}) fusion(bf16[16,2,1024,128]{2,3,1,0:T(8,128)(2,1)} %all-to-all-done), kind=kLoop, calls=%fused_computation.34 | loop fusion | bytes 16777216 | tf_op jit(solution)/shard_map/slice | solution.py:50
  164.6 6.4 %copy.19 = bf16[16,1,1024,128]{3,2,0,1:T(8,128)(2,1)} copy(bf16[16,1,1024,128]{2,3,1,0:T(8,128)(2,1)} %get-tuple-element.278) | data formatting | bytes 8388608
  171.0 6.4 %copy.18 = bf16[16,1,1024,128]{3,2,0,1:T(8,128)(2,1)} copy(bf16[16,1,1024,128]{2,3,1,0:T(8,128)(2,1)} %get-tuple-element.279) | data formatting | bytes 8388608
  177.4 65.6 %while.40 = (s32[]{:T(128)}, bf16[2,256,256]{2,1,0:T(8,128)(2,1)S(1)}, s32[2,256]{1,0:T(2,128)S(1)}, bf16[2,256,1,2,128]{4,3,1,2,0:T(2,128)(2,1)S(1)}, bf16[1638...) while((s32[]{:T(128)}, ...), condition=%wide.region_6.7_spmd, body=%wide.region_0.6_spmd.sunk | while | flops 550767872 | bytes 15816330 | solution.py:79
  180.7 29.2 %while.41 = (s32[]{:T(128)}, f32[1,512]{1,0:T(1,128)S(1)}, f32[1,512]{1,0:T(1,128)S(1)}, f32[1,512,128]{2,1,0:T(8,128)S(1)}, s32[]{:T(128)}, /*index=5*/bf16[163...) while((s32[]{:T(128)}, f32[1,512]{1,0:T(1,128)S(1)}, ...), condition=%wide.region_5.5_spmd.clone, body=%wide.region_2.4_spmd.clone.sunk | while | flops 550636544 | bytes 14365879 | solution.py:71
  184.1 2.4 fusion.39
  189.9 2.4 fusion.39
  192.7 2.2 fusion.37
  195.8 2.4 fusion.39
  198.5 2.2 fusion.37
  201.6 2.4 fusion.39
  204.4 2.2 fusion.37
  207.5 2.4 fusion.39
  213.5 29.2 %while.41 = (s32[]{:T(128)}, f32[1,512]{1,0:T(1,128)S(1)}, f32[1,512]{1,0:T(1,128)S(1)}, f32[1,512,128]{2,1,0:T(8,128)S(1)}, s32[]{:T(128)}, /*index=5*/bf16[163...) while((s32[]{:T(128)}, f32[1,512]{1,0:T(1,128)S(1)}, ...), condition=%wide.region_5.5_spmd.clone, body=%wide.region_2.4_spmd.clone.sunk | while | flops 550636544 | bytes 14365879 | solution.py:71
  216.9 2.4 fusion.39
  219.6 2.2 fusion.37
  222.8 2.4 fusion.39
  228.6 2.4 fusion.39
  231.3 2.2 fusion.37
  234.5 2.4 fusion.39
  240.3 2.4 fusion.39
  244.4 2.8 dynamic-slice_bitcast_fusion
  247.2 2.2 copy-done.1
  249.8 7.9 %collective-permute-done = f32[8,32,4608]{2,1,0:T(8,128)} collective-permute-done((f32[8,32,4608]{2,1,0:T(8,128)}, f32[8,32,4608]{2,1,0:T(8,128)}, u32[]{:S(2)}, u32[]{:S(2)}) %collective-permute-start) | collective-permute-done | bytes 4718624 | tf_op jit(solution)/shard_map/ppermute | solution.py:97
  257.7 4.3 %fusion.21 = bf16[8,32,4608]{2,1,0:T(8,128)(2,1)S(1)} fusion(f32[8,32,4608]{2,1,0:T(8,128)} %collective-permute-done, f32[8,2,32,4608]{3,2,1,0:T(8,128)} %copy-done.1, s32[]{:T(128)S(6)} %select_n.37), kind=kLoop, calls=%fused_computation.26 | loop fusion | flops 2359296 | bytes 11796484 | tf_op jit(solution)/shard_map/convert_element_type | solution.py:99
  262.0 45.9 %all_to_all.10 = bf16[8,32,4608]{2,1,0:T(8,128)(2,1)S(1)} all-to-all(bf16[8,32,4608]{2,1,0:T(8,128)(2,1)S(1)} %fusion.21), channel_id=1, replica_groups=mesh['pb'=8,'kx'=8,'kc'=2] {'kx'}, dimensions={0} | all-to-all | bytes 4718592 | tf_op jit(solution)/shard_map/all_to_all | solution.py:98
  (102 shorter events, 27.5 us)
Async XLA Ops:
  0.0 243.0 %copy-start = (bf16[256,4608]{1,0:T(8,128)(2,1)S(1)}, bf16[256,4608]{1,0:T(8,128)(2,1)}, u32[]{:S(2)}) copy-start(bf16[256,4608]{1,0:T(8,128)(2,1)} %param.13) | copy-start | bytes 7077892
  28.6 8.1 %copy-start.2 = (bf16[512,256]{1,0:T(8,128)(2,1)S(1)}, bf16[512,256]{1,0:T(8,128)(2,1)}, u32[]{:S(2)}) copy-start(bf16[512,256]{1,0:T(8,128)(2,1)} %param.10) | copy-start | bytes 786436
  28.6 129.9 %all-to-all-start = ((bf16[16,2,1024,128]{2,3,1,0:T(8,128)(2,1)}), bf16[16,2,1024,128]{2,3,1,0:T(8,128)(2,1)}, u32[]{:S(2)}, u32[]{:S(2)}) async-start(bf16[16,2,1024,128]{2,3,1,0:T(8,128)(2,1)} %copy.14), calls=%async_computation | async-start | bytes 16777216 | tf_op jit(solution)/shard_map/all_to_all | solution.py:48
  244.4 5.0 %copy-start.1 = (f32[8,2,32,4608]{3,2,1,0:T(8,128)}, f32[8,2,32,4608]{3,2,1,0:T(8,128)S(1)}, u32[]{:S(2)}) copy-start(f32[8,2,32,4608]{3,2,1,0:T(8,128)S(1)} %fusion.22) | copy-start | bytes 28311556
  249.4 8.3 %collective-permute-start = (f32[8,32,4608]{2,1,0:T(8,128)}, f32[8,32,4608]{2,1,0:T(8,128)}, u32[]{:S(2)}, u32[]{:S(2)}) collective-permute-start(f32[8,32,4608]{2,1,0:T(8,128)} %dynamic-slice_bitcast_fusion), channel_id=1, source_target_pairs={{0,1},{1,0},{2,3},{3,2},{4,5},{5,4},{6,7},{7,6},{8,9},{9,8},{10,11... | collective-permute-start | bytes 14155784 | tf_op jit(solution)/shard_map/ppermute | solution.py:97
